TPU v7x, 128 devices: a whole 4x4x4 slice. The times are simulated.
128 devices in a mesh: grp: 2 (over y_hi), row: 64 (over z, y_lo, x, core).
Axes of the slice: x: 4, y: 4 (y_hi: 2, y_lo: 2; y = y_hi * 2 + y_lo), z: 4, core: 2. Of those that a mesh axis runs over, the one named last changes fastest.
Arguments:
- features: bfloat16 [65536, 256], P(('grp', 'row')), may hold values from -6 to 6
- weight: bfloat16 [256, 256], replicated, may hold values from -0.375 to 0.375
- block_vals: bfloat16 [2, 512, 16, 128, 128], P('grp', 'row'), may hold values from -0.125 to 0.125
- block_cols: int32 [2, 512, 16], P('grp', 'row'), may hold values from 0 to 255, as said below
- block_count: int32 [2, 512], P('grp', 'row'), may hold values from 1 to 16, as said below
- cotangent: bfloat16 [65536, 256], P(('grp', 'row')), may hold values from -6 to 6
Outputs:
- activated: bfloat16 [65536, 256], P(('grp', 'row'))
- weight_grad: float32 [256, 256], replicated
- input_grad: bfloat16 [65536, 256], P(('grp', 'row'))
Inputs may be any that keep to these rules, and one draw needn't show every extreme that they name: `block_cols`: within one destination row block the 16 column blocks are distinct and ascending. `block_count`: in every draw some device holds 16 live slots in each of its row blocks.
All inputs are finite; a program needn't handle non-finite values.
Results may differ from a plain program's by a relative error of at most 0.0062.
Values may be sent and summed in bfloat16 or wider, within the bound.
No kernel may reach another device: no remote copies, remote signals or barrier semaphores. Data moves between devices by JAX's collectives and lax.ppermute only.
A program may use at most 128 MiB of HBM per device.

v0:
```python
import math
import jax
import jax.numpy as jnp
from jax import lax
from jax.sharding import PartitionSpec as P


def silu_slope(pre):
    sigma = jax.nn.sigmoid(pre)
    return sigma * (1.0 + pre * (1.0 - sigma))


def body(features, weight, block_vals, block_cols, block_count, cotangent):
    rows_dev, width = features.shape
    block = block_vals.shape[-1]
    slot_total = block_vals.shape[2]
    groups = lax.axis_size("grp")
    members = lax.axis_size("row")
    verts = rows_dev * groups * members
    slots = jnp.arange(slot_total)
    gathered = lax.all_gather(features, "row", axis=0, tiled=True)
    col_blocks = gathered.shape[0] // block
    panel_blocks = gathered.reshape(col_blocks, block, width)

    def aggregate(items):
        values, columns, count = items
        masked = jnp.where((slots < count)[:, None, None], values, jnp.zeros_like(values))
        picked = panel_blocks[columns]
        return jnp.einsum("kij,kjf->if", masked, picked, preferred_element_type=jnp.float32)

    partial_value = lax.map(aggregate, (block_vals[0], block_cols[0], block_count[0])).reshape(
        -1, width
    )
    summed = lax.psum_scatter(partial_value, "grp", scatter_dimension=0, tiled=True)
    aggregated = summed.astype(jnp.bfloat16)
    pre = jnp.dot(aggregated, weight, preferred_element_type=jnp.float32)
    activated = jax.nn.silu(pre).astype(jnp.bfloat16)
    pre_grad = (cotangent.astype(jnp.float32) * silu_slope(pre)).astype(jnp.bfloat16)
    local_grad = jnp.dot(aggregated.T, pre_grad, preferred_element_type=jnp.float32)
    own_grad = jnp.dot(pre_grad, weight.T, preferred_element_type=jnp.float32).astype(jnp.bfloat16)
    rows_grad = lax.all_gather(own_grad, "grp", axis=0, tiled=True)
    weight_grad = lax.psum(local_grad, ("grp", "row")) * (1.0 / math.sqrt(verts))
    by_block = rows_grad.reshape(-1, block, width)

    def spread(carry, items):
        values, columns, count, grad_block = items
        masked = jnp.where((slots < count)[:, None, None], values, jnp.zeros_like(values))
        contrib = jnp.einsum("kij,if->kjf", masked, grad_block, preferred_element_type=jnp.float32)
        return (carry.at[columns].add(contrib), None)

    total, unused = lax.scan(
        spread,
        jnp.zeros((col_blocks, block, width), jnp.float32),
        (block_vals[0], block_cols[0], block_count[0], by_block),
    )
    term = total.reshape(-1, width)
    input_grad = lax.psum_scatter(term, "row", scatter_dimension=0, tiled=True).astype(jnp.bfloat16)
    return (activated, weight_grad, input_grad)


def solution(mesh):
    placed = (
        P(("grp", "row"), None),
        P(),
        P("grp", "row", None, None, None),
        P("grp", "row", None),
        P("grp", "row"),
        P(("grp", "row"), None),
    )
    return jax.shard_map(
        body,
        mesh=mesh,
        in_specs=placed,
        out_specs=(P(("grp", "row"), None), P(), P(("grp", "row"), None)),
        check_vma=False,
    )
```

profile of v0, /device:TPU:0, one launch (start us, length us, event | category | flops | bytes accessed | tf_op | source)
XLA Modules:
  0.0 743.3 jit_solution(15940612499893916046)
XLA Ops:
  8.0 127.3 %all-gather.2.cloned.1.call-done = bf16[32768,256]{1,0:T(8,128)(2,1)} async-done(((bf16[512,256]{1,0:T(8,128)(2,1)}), bf16[32768,256]{1,0:T(8,128)(2,1)}) %all-gather.2.cloned.1.call-update) | async-done | bytes 16777232 | tf_op jit(solution)/shard_map/all_gather | solution.py:21
  135.3 88.4 %while.22 = (s32[]{:T(128)}, f32[8,128,256]{2,1,0:T(8,128)}, s32[8]{0:T(128)}, bf16[8,16,128,128]{3,2,1,0:T(8,128)(2,1)}, s32[8,16]{1,0:T(8,128)}, /*index=5*/bf16[256,128,256]{2,1,0:T(8,128)(2,1)}, s32[]{:T(128)}) while((s32[]{:T(128)}, f32[8,128,256]{2,1,0:T(8,128)}, s32[8]{0:T(128)}, bf16[8,16,128,128]{3,2,1,0:T(8,128)(2,1)}, ...), condition=%wide.region_1.2_spmd.clone, body=%wide.region_0.1_spmd.clone.sunk | while | flops 134480960 | bytes 3806601 | solution.py:31
  137.9 6.4 gather_fusion
  144.3 2.1 fusion.42
  148.9 6.4 gather_fusion
  155.3 2.1 fusion.42
  160.0 6.4 gather_fusion
  166.4 2.1 fusion.42
  171.0 6.4 gather_fusion
  177.4 2.1 fusion.42
  182.1 6.4 gather_fusion
  193.1 6.4 gather_fusion
  199.5 2.1 fusion.42
  204.1 6.4 gather_fusion
  210.5 2.1 fusion.42
  215.2 6.4 gather_fusion
  223.7 6.5 copy.9
  230.2 17.2 %reduce-scatter.3.cloned.1.call-done = f32[512,256]{1,0:T(8,128)} async-done(((f32[1024,256]{1,0:T(8,128)}), f32[512,256]{1,0:T(8,128)}) %reduce-scatter.3.cloned.1.call-update) | async-done | bytes 524304 | tf_op jit(solution)/shard_map/reduce_scatter | solution.py:34
  247.4 2.2 multiply_convert_fusion
  250.9 10.2 %all_gather.7 = bf16[1024,256]{1,0:T(8,128)(2,1)S(1)} all-gather(bf16[512,256]{1,0:T(8,128)(2,1)S(1)} %convolution_convert_fusion), channel_id=1, replica_groups=mesh['grp'=2,'row'=64] {'grp'}, dimensions={0}, use_global_device_ids=true | all-gather | bytes 786432 | tf_op jit(solution)/shard_map/all_gather | solution.py:41
  261.1 11.2 %broadcast_in_dim.28 = f32[256,128,256]{2,1,0:T(8,128)} broadcast(f32[]{:T(128)} %constant.27.clone.1), dimensions={} | broadcast | bytes 33554436 | tf_op jit(solution)/shard_map/broadcast_in_dim | solution.py:53
  272.4 63.8 %while.23 = (s32[]{:T(128)}, f32[256,128,256]{2,1,0:T(8,128)}, s32[8,16]{1,0:T(8,128)}, s32[8]{0:T(128)S(1)}, bf16[8,16,128,128]{2,3,1,0:T(8,128)(2,1)}, /*index=5*/bf16[8,128,256]{2,1,0:T(8,128)(2,1)S(1)}, s32[]{:T(128)}) while((s32[]{:T(128)}, f32[256,128,256]{2,1,0:T(8,128)}, s32[8,16]{1,0:T(8,128)}, s32[8]{0:T(128)S(1)}, ...), condition=%wide.region_6.7_spmd.clone, body=%wide.region_4.6_spmd.clone.sunk | while | flops 135004224 | bytes 8980281 | solution.py:51
  275.7 4.6 scatter_fusion
  283.7 4.6 scatter_fusion
  291.7 4.6 scatter_fusion
  299.7 4.6 scatter_fusion
  307.7 4.6 scatter_fusion
  315.7 4.6 scatter_fusion
  323.6 4.6 scatter_fusion
  331.6 4.6 scatter_fusion
  336.2 58.5 %all-reduce.2.cloned.1.call-done = f32[256,256]{1,0:T(8,128)} async-done(((f32[256,256]{1,0:T(8,128)}), f32[256,256]{1,0:T(8,128)}) %all-reduce.2.cloned.1.call-update) | async-done | bytes 262160 | tf_op jit(solution)/shard_map/psum | solution.py:42
  396.5 338.6 %reduce-scatter.5.cloned.1.call-done = f32[512,256]{1,0:T(8,128)} async-done(((f32[32768,256]{1,0:T(8,128)}), f32[512,256]{1,0:T(8,128)}) %reduce-scatter.5.cloned.1.call-update) | async-done | bytes 524304 | tf_op jit(solution)/shard_map/reduce_scatter | solution.py:57
  (87 shorter events, 57.2 us)
Async XLA Ops:
  7.2 240.2 %copy-start = (bf16[256,256]{1,0:T(8,128)(2,1)S(1)}, bf16[256,256]{1,0:T(8,128)(2,1)}, u32[]{:S(2)}) copy-start(bf16[256,256]{1,0:T(8,128)(2,1)} %param.11) | copy-start | bytes 393220
  7.2 128.1 %all-gather.2.cloned.1.call-start = ((), (), s32[]{:S(2)}) async-start(), calls=%async_computation.2 | async-start | bytes 17039360 | tf_op jit(solution)/shard_map/all_gather | solution.py:21
  7.9 239.5 %reduce-scatter.3.cloned.1.call-start = ((), (), s32[]{:S(2)}) async-start(), calls=%async_computation.3 | async-start | bytes 1572864 | tf_op jit(solution)/shard_map/reduce_scatter | solution.py:34
  223.7 23.7 %copy-start.2 = (bf16[512,256]{1,0:T(8,128)(2,1)S(1)}, bf16[512,256]{1,0:T(8,128)(2,1)}, u32[]{:S(2)}) copy-start(bf16[512,256]{1,0:T(8,128)(2,1)} %param.15) | copy-start | bytes 786436
  223.7 171.1 %all-reduce.2.cloned.1.call-start = ((), (), s32[]{:S(2)}) async-start(), calls=%async_computation.4 | async-start | bytes 524288 | tf_op jit(solution)/shard_map/psum | solution.py:42
  247.4 2.5 copy-start.1
  250.9 484.1 %reduce-scatter.5.cloned.1.call-start = ((), (), s32[]{:S(2)}) async-start(), calls=%async_computation.5 | async-start | bytes 34078720 | tf_op jit(solution)/shard_map/reduce_scatter | solution.py:57
  261.1 11.2 %copy-start.3 = (s32[8]{0:T(128)S(1)}, s32[8]{0:T(128)}, u32[]{:S(2)}) copy-start(s32[8]{0:T(128)} %get-tuple-element.273) | copy-start | bytes 100
Sparse Core Ops, SparseCore 0:
  9.7 125.4 all-gather.1
  223.8 23.5 reduce-scatter.2
  253.4 141.3 all-reduce.1
  397.2 337.8 reduce-scatter.4
where the time goes:
time: 746 us; the launch traced here: 743 us
  waiting for transfers between devices  542 us (73%)
  local copies, waits for them, and re-layouts  83.3 us (11%)
  other arithmetic  61.3 us (8%)
  matrix products  32 us (4%)
  between operations  13.8 us (2%)
  blocking collectives  10.2 us (1%)
    reduce_scatter x1, waiting for transfers between devices, body(): lax.psum_scatter(term, 'row', scatter_dimension=0, tiled=True)  339 us
    all_gather x1, waiting for transfers between devices, body(): gathered = lax.all_gather(features, 'row', axis=0, tiled=True)  127 us
    psum x1, waiting for transfers between devices, body(): lax.psum(local_grad, ('grp', 'row')) * (1.0 / math.sqrt(verts))  58.5 us
    gather x8, local copies, waits for them, and re-layouts, aggregate(): picked = panel_blocks[columns]  51.1 us
    scatter-add x8, other arithmetic, spread(): return (carry.at[columns].add(contrib), None)  36.9 us
    reduce_scatter x1, waiting for transfers between devices, body(): lax.psum_scatter(partial_value, 'grp', scatter_dimension=0, tiled=True)  17.2 us
    dot_general x8, matrix products, aggregate(): jnp.einsum('kij,kjf->if', masked, picked, preferred_element_type=jnp.floa...  16.4 us
  transfers between devices with their start and end apart: 4, of which 4 were waited for; matrix products, arithmetic and copies ran while one was open for 11% of the time, Pallas kernels for 0%

commit v1 on v0

--- a/solution.py
+++ b/solution.py
@@ -1,8 +1,18 @@
+import functools
 import math
 import jax
 import jax.numpy as jnp
 from jax import lax
 from jax.sharding import PartitionSpec as P
+
+
+def sites_follow(my_data, chip_axis, axis_id):
+    for k0 in (chip_axis, axis_id):
+        my_data = lax.psum(my_data, axis_name=k0)
+    return my_data
+
+
+body_order = functools.partial(sites_follow, chip_axis="grp", axis_id="row")
 
 
 def silu_slope(pre):
@@ -39,7 +49,7 @@
     local_grad = jnp.dot(aggregated.T, pre_grad, preferred_element_type=jnp.float32)
     own_grad = jnp.dot(pre_grad, weight.T, preferred_element_type=jnp.float32).astype(jnp.bfloat16)
     rows_grad = lax.all_gather(own_grad, "grp", axis=0, tiled=True)
-    weight_grad = lax.psum(local_grad, ("grp", "row")) * (1.0 / math.sqrt(verts))
+    weight_grad = body_order(local_grad) * (1.0 / math.sqrt(verts))
     by_block = rows_grad.reshape(-1, block, width)
 
     def spread(carry, items):

time: 746 us -> 1140 us (1.53)
  waiting for transfers between devices: 542 us -> 931 us
    psum x1 -> x2, waiting for transfers between devices: 58.5 us -> 447 us  [sites_follow(): my_data = lax.psum(my_data, axis_name=k0)]
  transfers between devices with their start and end apart: 4 -> 5, of which waited for: 4 -> 5; matrix products, arithmetic and copies ran while one was open for 11% -> 7% of each run, Pallas kernels for 0% -> 0%
where the time goes in v1:
time: 1140 us; the launch traced here: 1130 us
  waiting for transfers between devices  931 us (82%)
  local copies, waits for them, and re-layouts  83.4 us (7%)
  other arithmetic  62 us (5%)
  matrix products  32.9 us (3%)
  between operations  13.8 us (1%)
    psum x2, waiting for transfers between devices, sites_follow(): my_data = lax.psum(my_data, axis_name=k0)  447 us
    reduce_scatter x1, waiting for transfers between devices, body(): lax.psum_scatter(term, 'row', scatter_dimension=0, tiled=True)  339 us
    all_gather x1, waiting for transfers between devices, body(): gathered = lax.all_gather(features, 'row', axis=0, tiled=True)  127 us
    gather x8, local copies, waits for them, and re-layouts, aggregate(): picked = panel_blocks[columns]  51.1 us
    scatter-add x8, other arithmetic, spread(): return (carry.at[columns].add(contrib), None)  36.9 us
  transfers between devices with their start and end apart: 5, of which 5 were waited for; matrix products, arithmetic and copies ran while one was open for 7% of the time, Pallas kernels for 0%

profile of v1, /device:TPU:0, one launch (start us, length us, event | category | flops | bytes accessed | tf_op | source)
XLA Modules:
  0.0 1133.8 jit_solution(7264399422172430454)
XLA Ops:
  8.0 127.3 %all-gather.2.cloned.1.call-done = bf16[32768,256]{1,0:T(8,128)(2,1)} async-done(((bf16[512,256]{1,0:T(8,128)(2,1)}), bf16[32768,256]{1,0:T(8,128)(2,1)}) %all-gather.2.cloned.1.call-update) | async-done | bytes 16777232 | tf_op jit(solution)/shard_map/all_gather | solution.py:31
  135.3 88.4 %while.22 = (s32[]{:T(128)}, f32[8,128,256]{2,1,0:T(8,128)}, s32[8]{0:T(128)}, bf16[8,16,128,128]{3,2,1,0:T(8,128)(2,1)}, s32[8,16]{1,0:T(8,128)}, /*index=5*/bf16[256,128,256]{2,1,0:T(8,128)(2,1)}, s32[]{:T(128)}) while((s32[]{:T(128)}, f32[8,128,256]{2,1,0:T(8,128)}, s32[8]{0:T(128)}, bf16[8,16,128,128]{3,2,1,0:T(8,128)(2,1)}, ...), condition=%wide.region_1.2_spmd.clone, body=%wide.region_0.1_spmd.clone.sunk | while | flops 134480960 | bytes 3806601 | solution.py:41
  137.9 6.4 gather_fusion
  144.3 2.1 fusion.42
  148.9 6.4 gather_fusion
  155.3 2.1 fusion.42
  160.0 6.4 gather_fusion
  166.4 2.1 fusion.42
  171.0 6.4 gather_fusion
  177.4 2.1 fusion.42
  182.1 6.4 gather_fusion
  193.1 6.4 gather_fusion
  204.1 6.4 gather_fusion
  210.5 2.1 fusion.42
  215.2 6.4 gather_fusion
  223.7 6.5 copy.9
  230.2 17.2 %reduce-scatter.3.cloned.1.call-done = f32[512,256]{1,0:T(8,128)} async-done(((f32[1024,256]{1,0:T(8,128)}), f32[512,256]{1,0:T(8,128)}) %reduce-scatter.3.cloned.1.call-update) | async-done | bytes 524304 | tf_op jit(solution)/shard_map/reduce_scatter | solution.py:44
  247.4 2.1 multiply_convert_fusion
  251.9 10.2 all_gather.7
  262.1 20.3 %all-reduce.3.cloned.1.call-done = f32[256,256]{1,0:T(8,128)} async-done(((f32[256,256]{1,0:T(8,128)}), f32[256,256]{1,0:T(8,128)}) %all-reduce.3.cloned.1.call-update) | async-done | bytes 262160 | tf_op jit(solution)/shard_map/psum | solution.py:11
  282.5 11.2 broadcast_in_dim.28
  293.7 64.6 %while.23 = (s32[]{:T(128)}, f32[256,128,256]{2,1,0:T(8,128)}, s32[8,16]{1,0:T(8,128)}, s32[8]{0:T(128)S(1)}, bf16[8,16,128,128]{2,3,1,0:T(8,128)(2,1)}, /*index=5*/bf16[8,128,256]{2,1,0:T(8,128)(2,1)S(1)}, s32[]{:T(128)}) while((s32[]{:T(128)}, f32[256,128,256]{2,1,0:T(8,128)}, s32[8,16]{1,0:T(8,128)}, s32[8]{0:T(128)S(1)}, ...), condition=%wide.region_7.8_spmd.clone, body=%wide.region_5.7_spmd.clone.sunk | while | flops 135004224 | bytes 8980281 | solution.py:61
  297.2 4.6 scatter_fusion
  305.3 4.6 scatter_fusion
  313.4 4.6 scatter_fusion
  321.4 4.6 scatter_fusion
  329.5 4.6 scatter_fusion
  337.6 4.6 scatter_fusion
  345.6 4.6 scatter_fusion
  353.7 4.6 scatter_fusion
  358.3 426.9 %all-reduce.5.cloned.1.call-done = f32[256,256]{1,0:T(8,128)} async-done(((f32[256,256]{1,0:T(8,128)}), f32[256,256]{1,0:T(8,128)}) %all-reduce.5.cloned.1.call-update) | async-done | bytes 262160 | tf_op jit(solution)/shard_map/psum | solution.py:11
  786.9 338.6 %reduce-scatter.5.cloned.1.call-done = f32[512,256]{1,0:T(8,128)} async-done(((f32[32768,256]{1,0:T(8,128)}), f32[512,256]{1,0:T(8,128)}) %reduce-scatter.5.cloned.1.call-update) | async-done | bytes 524304 | tf_op jit(solution)/shard_map/reduce_scatter | solution.py:67
  (90 shorter events, 61.1 us)
Async XLA Ops:
  7.2 240.2 %copy-start = (bf16[256,256]{1,0:T(8,128)(2,1)S(1)}, bf16[256,256]{1,0:T(8,128)(2,1)}, u32[]{:S(2)}) copy-start(bf16[256,256]{1,0:T(8,128)(2,1)} %param.11) | copy-start | bytes 393220
  7.2 128.1 %all-gather.2.cloned.1.call-start = ((), (), s32[]{:S(2)}) async-start(), calls=%async_computation.2 | async-start | bytes 17039360 | tf_op jit(solution)/shard_map/all_gather | solution.py:31
  7.9 239.5 %reduce-scatter.3.cloned.1.call-start = ((), (), s32[]{:S(2)}) async-start(), calls=%async_computation.3 | async-start | bytes 1572864 | tf_op jit(solution)/shard_map/reduce_scatter | solution.py:44
  223.7 23.7 %copy-start.2 = (bf16[512,256]{1,0:T(8,128)(2,1)S(1)}, bf16[512,256]{1,0:T(8,128)(2,1)}, u32[]{:S(2)}) copy-start(bf16[512,256]{1,0:T(8,128)(2,1)} %param.15) | copy-start | bytes 786436
  223.7 58.7 %all-reduce.3.cloned.1.call-start = ((), (), s32[]{:S(2)}) async-start(), calls=%async_computation.4 | async-start | bytes 524288 | tf_op jit(solution)/shard_map/psum | solution.py:11
  251.6 533.7 %all-reduce.5.cloned.1.call-start = ((), (), s32[]{:S(2)}) async-start(), calls=%async_computation.5 | async-start | bytes 524288 | tf_op jit(solution)/shard_map/psum | solution.py:11
  282.4 843.1 %reduce-scatter.5.cloned.1.call-start = ((), (), s32[]{:S(2)}) async-start(), calls=%async_computation.6 | async-start | bytes 34078720 | tf_op jit(solution)/shard_map/reduce_scatter | solution.py:67
  282.5 11.3 copy-start.3
  358.3 769.0 %copy-start.1 = (bf16[256,256]{1,0:T(8,128)(2,1)S(1)}, bf16[256,256]{1,0:T(8,128)(2,1)}, u32[]{:S(2)}) copy-start(bf16[256,256]{1,0:T(8,128)(2,1)} %param.11) | copy-start | bytes 393220
Sparse Core Ops, SparseCore 0:
  9.7 125.4 all-gather.1
  223.8 23.5 reduce-scatter.2
  251.7 30.6 all-reduce.2
  284.7 500.4 all-reduce.4
  787.6 337.8 reduce-scatter.4
